TPU v7x, 32 devices: a whole 2x2x4 slice. The times are simulated.
32 devices in a mesh: groups: 2 (over y), lat: 8 (over z, x), seed: 2 (over core).
Axes of the slice: x: 2, y: 2, z: 4, core: 2. Of those that a mesh axis runs over, the one named last changes fastest.
Arguments:
- activations: bfloat16 [512, 2048], P(('groups', 'seed'), 'lat'), parts along dimension 0, may hold values from -6 to 6
- bag_rows: int32 [4, 256], P(('groups', 'seed')), parts along dimension 0, may hold values from 0 to 255
- keep_cols: int32 [4, 2048], P(('groups', 'seed')), parts along dimension 0, may hold values 0 or 1
- enc_weight: bfloat16 [4, 16384, 2048], P(('groups', 'seed'), 'lat'), parts along dimension 0, may hold values from -0.125 to 0.125
- enc_bias: float32 [4, 16384], P(('groups', 'seed'), 'lat'), parts along dimension 0, may hold values from -3 to 3
- dec_weight: bfloat16 [4, 16384, 2048], P(('groups', 'seed'), 'lat'), parts along dimension 0, may hold values from -0.0625 to 0.0625
- dec_bias: float32 [4, 2048], P(('groups', 'seed')), parts along dimension 0, may hold values from -3 to 3
- first_moment: bfloat16 [4, 16384, 2048], P(('groups', 'seed'), 'lat'), parts along dimension 0, may hold values from -0.3125 to 0.3125
- second_moment: bfloat16 [4, 16384, 2048], P(('groups', 'seed'), 'lat'), parts along dimension 0, may hold values from 9.9658966e-05 to 0.0099487305
Outputs:
- new_weight: bfloat16 [4, 16384, 2048], P(('groups', 'seed'), 'lat'), parts along dimension 0
- new_first: bfloat16 [4, 16384, 2048], P(('groups', 'seed'), 'lat'), parts along dimension 0
- new_second: bfloat16 [4, 16384, 2048], P(('groups', 'seed'), 'lat'), parts along dimension 0
There are 2 independent parts, one for each index of `groups`. A program takes and returns all parts, laid end to end along the dimension named above; each array names one. Nothing has to cross between parts.
All inputs are finite; a program needn't handle non-finite values. No bound on the sum of `keep_cols` on one device may be relied on, other than what follows from the above.
Results may differ from a plain program's by a relative error of at most 0.012.
The roundings to bfloat16 on the way count: a program that leaves them out, or rounds other values in their place, can miss the bound.
Values may be sent and summed in bfloat16 or wider, within the bound.
No kernel may reach another device: no remote copies, remote signals or barrier semaphores. Data moves between devices by JAX's collectives and lax.ppermute only.
A program may use at most 128 MiB of HBM per device.

v0:
```python
import jax
import jax.numpy as jnp
from jax import lax
from jax.sharding import PartitionSpec as P

sparsity = 0.2
beta_one = 0.9
beta_two = 0.95
corr_one = 1.0 - 0.9**10
corr_two = 1.0 - 0.95**10
adam_eps = 1e-08
rate_step = 0.001
decay_rate = 0.1


def local(
    activations,
    bag_rows,
    keep_cols,
    enc_weight,
    enc_bias,
    dec_weight,
    dec_bias,
    first_moment,
    second_moment,
):
    half_rows = lax.all_gather(activations, "lat", axis=1, tiled=True)
    gathered = lax.all_gather(half_rows, "seed", axis=0, tiled=True)
    row_order = bag_rows[0]
    sample = jnp.take(gathered, row_order, axis=0)
    weight_in = enc_weight[0]
    decoder = dec_weight[0]
    bias_dec = dec_bias[0]
    keep = keep_cols[0].astype(jnp.float32)
    centered = (sample.astype(jnp.float32) - bias_dec).astype(jnp.bfloat16)
    pre_t = lax.dot_general(
        weight_in, centered, (((1,), (1,)), ((), ())), preferred_element_type=jnp.float32
    )
    pre_t = pre_t + enc_bias[0][:, None]
    latent_t = jnp.maximum(pre_t, 0.0).astype(jnp.bfloat16)
    partial_sum = lax.dot_general(
        latent_t, decoder, (((0,), (0,)), ((), ())), preferred_element_type=jnp.float32
    )
    total = lax.psum(partial_sum, "lat")
    error = ((total + bias_dec - sample.astype(jnp.float32)) * keep).astype(jnp.bfloat16)
    back_t = lax.dot_general(
        decoder, error, (((1,), (1,)), ((), ())), preferred_element_type=jnp.float32
    )
    row_norm = jnp.sqrt(jnp.sum(jnp.square(decoder.astype(jnp.float32)), axis=1) + 1e-06)
    token_total = sample.shape[0]
    d_pre_t = (
        jnp.where(pre_t > 0, 2.0 * back_t + sparsity * row_norm[:, None], 0.0) / token_total
    ).astype(jnp.bfloat16)
    grad = jnp.dot(d_pre_t, centered, preferred_element_type=jnp.float32)
    moment_one = beta_one * first_moment[0].astype(jnp.float32) + (1.0 - beta_one) * grad
    moment_two = beta_two * second_moment[0].astype(jnp.float32) + (1.0 - beta_two) * grad * grad
    direction = moment_one / corr_one / (jnp.sqrt(moment_two / corr_two) + adam_eps)
    old = weight_in.astype(jnp.float32)
    updated = (old - rate_step * (direction + decay_rate * old)).astype(jnp.bfloat16)
    return (
        updated[None],
        moment_one.astype(jnp.bfloat16)[None],
        moment_two.astype(jnp.bfloat16)[None],
    )


def solution(mesh):
    return jax.shard_map(
        local,
        mesh=mesh,
        in_specs=(
            P(("groups", "seed"), "lat"),
            P(("groups", "seed"), None),
            P(("groups", "seed"), None),
            P(("groups", "seed"), "lat", None),
            P(("groups", "seed"), "lat"),
            P(("groups", "seed"), "lat", None),
            P(("groups", "seed"), None),
            P(("groups", "seed"), "lat", None),
            P(("groups", "seed"), "lat", None),
        ),
        out_specs=(
            P(("groups", "seed"), "lat", None),
            P(("groups", "seed"), "lat", None),
            P(("groups", "seed"), "lat", None),
        ),
        check_vma=False,
    )
```

profile of v0, /device:TPU:0, one launch (start us, length us, event | category | flops | bytes accessed | tf_op | source)
XLA Modules:
  0.0 222.0 jit_solution(16715430085450274316)
XLA Ops:
  7.2 0.0 copy-start
  7.2 0.0 copy-start.2
  7.2 0.0 all-gather.2.cloned.1.call-start
  7.2 35.4 %all_gather.6 = bf16[128,2048]{1,0:T(8,128)(2,1)} all-gather(bf16[128,256]{1,0:T(8,128)(2,1)} %param.9), channel_id=1, replica_groups=mesh['groups'=2,'lat'=8,'seed'=2] {'lat'}, dimensions={1}, use_global_device_ids=true | all-gather | bytes 589824 | tf_op jit(solution)/shard_map/all_gather | solution.py:27
  42.6 0.0 all-gather.2.cloned.1.call-update
  42.7 0.0 all-reduce.2.cloned.1.call-start
  42.7 0.7 compare_select_fusion
  43.4 0.7 compare_and_fusion
  44.1 8.8 %all-gather.2.cloned.1.call-done = bf16[256,2048]{1,0:T(8,128)(2,1)} async-done(((bf16[128,2048]{1,0:T(8,128)(2,1)}), bf16[256,2048]{1,0:T(8,128)(2,1)}) %all-gather.2.cloned.1.call-update) | async-done | bytes 1048592 | tf_op jit(solution)/shard_map/all_gather | solution.py:28
  52.9 3.7 %gather_fusion = bf16[256,2048]{1,0:T(8,128)(2,1)S(1)} fusion(bf16[256,2048]{1,0:T(8,128)(2,1)} %all-gather.2.cloned.1.call-done, s32[1024]{0:T(1024)S(1)} %pad_clamp_fusion), kind=kCustom, calls=%fused_computation | custom fusion | bytes 2098176 | tf_op jit(solution)/shard_map/jit(_take)/gather | solution.py:30
  56.6 0.0 copy-done
  56.6 0.0 copy-done.2
  56.7 5.8 %fusion.27 = f32[256,2048]{1,0:T(8,128)S(1)} fusion(bf16[1,2048,2048]{2,1,0:T(8,128)(2,1)} %param.12, f32[2048]{0:T(1024)S(1)} %bitcast.64, f32[2048]{0:T(1024)S(1)} %bitcast.59, bf16[256,2048]{1,0:T(8,128)(2,1)S(1)} %gather_fusion, pred[256]{0:T(512)(128)(4,1)S(1)} %compare_and_fusion), kind=kOutput, calls=%fused_computation.27 | convolution fusion | flops 2150105088 | bytes 11550976 | tf_op jit(solution)/shard_map/dot_general | solution.py:36
  62.4 0.0 copy-start.1
  62.5 7.0 %fusion.10 = f32[256,2048]{1,0:T(8,128)} fusion(bf16[1,2048,2048]{2,1,0:T(8,128)(2,1)} %param.14, f32[256,2048]{1,0:T(8,128)S(1)} %fusion.27), kind=kOutput, calls=%fused_computation.16 | convolution fusion | flops 2148532224 | bytes 12582912 | tf_op jit(solution)/shard_map/dot_general | solution.py:41
  69.5 0.0 all-reduce.2.cloned.1.call-update
  69.5 0.0 copy-done.1
  69.5 5.1 %multiply_reduce_fusion = f32[2048]{0:T(1024)S(1)} fusion(bf16[1,2048,2048]{2,1,0:T(8,128)(2,1)} %param.14), kind=kLoop, calls=%fused_computation.9 | loop fusion | flops 12580864 | bytes 8396800 | tf_op jit(solution)/shard_map/reduce_sum | solution.py:49
  74.6 98.0 %all-reduce.2.cloned.1.call-done = f32[256,2048]{1,0:T(8,128)} async-done(((f32[256,2048]{1,0:T(8,128)}), f32[256,2048]{1,0:T(8,128)}) %all-reduce.2.cloned.1.call-update) | async-done | bytes 2097168 | tf_op jit(solution)/shard_map/psum | solution.py:44
  172.7 14.7 %fusion.34 = f32[2048,2048]{1,0:T(8,128)} fusion(bf16[1,2048,2048]{2,1,0:T(8,128)(2,1)} %param.14, f32[256,2048]{1,0:T(8,128)S(1)} %fusion.27, f32[256,2048]{1,0:T(8,128)} %all-reduce.2.cloned.1.call-done, f32[2048]{0:T(1024)S(1)} %sqrt_multiply_fusion, f32[2048]{0:T(1024)S(1)} %bitcast.61, f32[2048]{0:T(1024)S(1)} %bitcast.60, ...), kind=kOutput, calls=%fused_computation.29 | convolution fusion | flops 4303355904 | bytes 30433536 | tf_op jit(solution)/shard_map/dot_general | solution.py:54
  187.3 27.9 %fusion.6 = (bf16[1,2048,2048]{2,1,0:T(8,128)(2,1)}, bf16[1,2048,2048]{2,1,0:T(8,128)(2,1)}, bf16[1,2048,2048]{2,1,0:T(8,128)(2,1)}) fusion(f32[2048,2048]{1,0:T(8,128)} %fusion.34, bf16[1,2048,2048]{2,1,0:T(8,128)(2,1)} %param.17, bf16[1,2048,2048]{2,1,0:T(8,128)(2,1)} %param.16, bf16[1,2048,2048]{2,1,0:T(8,128)(2,1)} %param.12), kind=kLoop, calls=%fused_computation.12 | loop fusion | flops 88080384 | bytes 67108864 | tf_op jit(solution)/shard_map/broadcast_in_dim | solution.py:63
  (3 shorter events, 0.0 us)
Async XLA Ops:
  7.2 49.5 %copy-start = (f32[1,2048]{1,0:T(1,128)S(1)}, f32[1,2048]{1,0:T(1,128)}, u32[]{:S(2)}) copy-start(f32[1,2048]{1,0:T(1,128)} %param.15) | copy-start | bytes 24580
  7.2 49.5 %copy-start.2 = (f32[1,2048]{1,0:T(1,128)S(1)}, f32[1,2048]{1,0:T(1,128)}, u32[]{:S(2)}) copy-start(f32[1,2048]{1,0:T(1,128)} %param.13) | copy-start | bytes 24580
  7.2 45.7 %all-gather.2.cloned.1.call-start = ((), (), s32[]{:S(2)}) async-start(), calls=%async_computation | async-start | bytes 1572864 | tf_op jit(solution)/shard_map/all_gather | solution.py:28
  42.7 130.0 %all-reduce.2.cloned.1.call-start = ((), (), s32[]{:S(2)}) async-start(), calls=%async_computation.1 | async-start | bytes 4194304 | tf_op jit(solution)/shard_map/psum | solution.py:44
  62.4 7.1 %copy-start.1 = (s32[1,2048]{1,0:T(1,128)S(1)}, s32[1,2048]{1,0:T(1,128)}, u32[]{:S(2)}) copy-start(s32[1,2048]{1,0:T(1,128)} %param.11) | copy-start | bytes 24580
Sparse Core Ops, SparseCore 0:
  42.8 10.0 all-gather.1
  69.6 103.0 all-reduce.1
where the time goes:
time: 222 us
  waiting for transfers between devices  107 us (48%)
  blocking collectives  35.4 us (16%)
  other arithmetic  34.3 us (15%)
  matrix products  27.5 us (12%)
  between operations  14.1 us (6%)
  local copies, waits for them, and re-layouts  3.74 us (2%)
    psum x1, waiting for transfers between devices, local(): total = lax.psum(partial_sum, 'lat')  98 us
    all_gather x1, blocking collectives, local(): half_rows = lax.all_gather(activations, 'lat', axis=1, tiled=True)  35.4 us
    broadcast_in_dim x1, other arithmetic, local(): moment_two.astype(jnp.bfloat16)[None]  27.9 us
    dot_general x1, matrix products, local(): grad = jnp.dot(d_pre_t, centered, preferred_element_type=jnp.float32)  14.7 us
    all_gather x1, waiting for transfers between devices, local(): gathered = lax.all_gather(half_rows, 'seed', axis=0, tiled=True)  8.8 us
    dot_general x1, matrix products, local(): lax.dot_general(latent_t, decoder, (((0,), (0,)), ((), ())), preferred_el...  7.04 us
    dot_general x1, matrix products, local(): lax.dot_general(weight_in, centered, (((1,), (1,)), ((), ())), preferred_...  5.77 us
    reduce_sum x1, other arithmetic, local(): jnp.sum(jnp.square(decoder.astype(jnp.float32)), axis=1) + 1e-06  5.08 us
  transfers between devices with their start and end apart: 2, of which 2 were waited for; matrix products, arithmetic and copies ran while one was open for 3% of the time, Pallas kernels for 0%

commit v1 on v0

--- a/solution.py
+++ b/solution.py
@@ -1,7 +1,9 @@
+import functools
 import jax
 import jax.numpy as jnp
 from jax import lax
 from jax.sharding import PartitionSpec as P
+from jax.lax import axis_index, axis_size, ppermute
 
 sparsity = 0.2
 beta_one = 0.9
@@ -11,6 +13,33 @@
 adam_eps = 1e-08
 rate_step = 0.001
 decay_rate = 0.1
+
+
+def _raise_islands(vals, dimension_no):
+    row_out = list(vals.shape[1:])
+    row_out[dimension_no] *= vals.shape[0]
+    return jnp.moveaxis(vals, 0, dimension_no).reshape(row_out)
+
+
+def task_supply(u_in, bus_axis):
+    before = u_in[None]
+    num_devices = axis_size(bus_axis)
+    for j0 in range(num_devices.bit_length() - 1):
+        built = 1 << j0
+        all_values = ppermute(
+            before, bus_axis, tuple(((nth, nth ^ built) for nth in range(num_devices)))
+        )
+        z_new = jnp.stack([before, all_values], 0)
+        local_next = axis_index(bus_axis) >> j0 & 1
+        before = jnp.where(local_next == 0, z_new, z_new[::-1]).reshape(-1, *u_in.shape)
+    return before
+
+
+def _shape_strips_all(base_x, q_in, dim_at):
+    return _raise_islands(task_supply(base_x, q_in), dim_at)
+
+
+search_lane = functools.partial(_shape_strips_all, q_in="lat", dim_at=1)
 
 
 def local(
@@ -24,7 +53,7 @@
     first_moment,
     second_moment,
 ):
-    half_rows = lax.all_gather(activations, "lat", axis=1, tiled=True)
+    half_rows = search_lane(activations)
     gathered = lax.all_gather(half_rows, "seed", axis=0, tiled=True)
     row_order = bag_rows[0]
     sample = jnp.take(gathered, row_order, axis=0)

time: 222 us -> 212 us (0.955)
  blocking collectives: 35.4 us -> 0 us
  waiting for transfers between devices: 107 us -> 122 us
  starting transfers between devices: 0.08 us -> 8.35 us
    all_gather x1 -> x0, blocking collectives: 35.4 us -> none  [local(): half_rows = lax.all_gather(activations, 'lat', axis=1, tiled=True)]
    ppermute x0 -> x3, waiting for transfers between devices: none -> 15 us  [task_supply(): ppermute(before, bus_axis, tuple(((nth, nth ^ built) for nth in range(num...]
    ppermute x0 -> x3, starting transfers between devices: none -> 8.27 us  [task_supply(): ppermute(before, bus_axis, tuple(((nth, nth ^ built) for nth in range(num...]
  transfers between devices with their start and end apart: 2 -> 5, of which waited for: 2 -> 5; matrix products, arithmetic and copies ran while one was open for 3% -> 3% of each run, Pallas kernels for 0% -> 0%
where the time goes in v1:
time: 212 us
  waiting for transfers between devices  122 us (58%)
  other arithmetic  35.4 us (17%)
  matrix products  27.5 us (13%)
  between operations  14.1 us (7%)
  starting transfers between devices  8.35 us (4%)
  local copies, waits for them, and re-layouts  4.58 us (2%)
    psum x1, waiting for transfers between devices, local(): total = lax.psum(partial_sum, 'lat')  97.9 us
    broadcast_in_dim x1, other arithmetic, local(): moment_two.astype(jnp.bfloat16)[None]  27.9 us
    ppermute x3, waiting for transfers between devices, task_supply(): ppermute(before, bus_axis, tuple(((nth, nth ^ built) for nth in range(num...  15 us
    dot_general x1, matrix products, local(): grad = jnp.dot(d_pre_t, centered, preferred_element_type=jnp.float32)  14.7 us
    all_gather x1, waiting for transfers between devices, local(): gathered = lax.all_gather(half_rows, 'seed', axis=0, tiled=True)  8.95 us
    ppermute x3, starting transfers between devices, task_supply(): ppermute(before, bus_axis, tuple(((nth, nth ^ built) for nth in range(num...  8.27 us
    dot_general x1, matrix products, local(): lax.dot_general(latent_t, decoder, (((0,), (0,)), ((), ())), preferred_el...  7.04 us
    dot_general x1, matrix products, local(): lax.dot_general(weight_in, centered, (((1,), (1,)), ((), ())), preferred_...  5.77 us
  transfers between devices with their start and end apart: 5, of which 5 were waited for; matrix products, arithmetic and copies ran while one was open for 3% of the time, Pallas kernels for 0%

profile of v1, /device:TPU:0, one launch (start us, length us, event | category | flops | bytes accessed | tf_op | source)
XLA Modules:
  0.0 212.0 jit_solution(11551554040054196578)
XLA Ops:
  7.2 0.0 copy-start
  7.2 0.0 copy-start.2
  7.2 0.0 all-gather.2.cloned.1.call-start
  7.2 3.0 %collective-permute-start = (bf16[1,128,256]{2,1,0:T(8,128)(2,1)}, bf16[1,128,256]{2,1,0:T(8,128)(2,1)S(1)}, u32[]{:S(2)}, u32[]{:S(2)}) collective-permute-start(bf16[1,128,256]{2,1,0:T(8,128)(2,1)} %bitcast.85), channel_id=1, source_target_pairs={{0,2},{2,0},{4,6},{6,4},{8,10},{10,8},{12,14},{14,12},{1,3},{3,1},... | collective-permute-start | bytes 196616 | tf_op jit(solution)/shard_map/ppermute | solution.py:29
  10.2 2.5 %collective-permute-done = bf16[1,128,256]{2,1,0:T(8,128)(2,1)S(1)} collective-permute-done((bf16[1,128,256]{2,1,0:T(8,128)(2,1)}, bf16[1,128,256]{2,1,0:T(8,128)(2,1)S(1)}, u32[]{:S(2)}, u32[]{:S(2)}) %collective-permute-start) | collective-permute-done | bytes 65568 | tf_op jit(solution)/shard_map/ppermute | solution.py:29
  12.7 0.9 pad_maximum_fusion.2
  13.6 2.2 %collective-permute-start.1 = (bf16[2,128,256]{2,1,0:T(8,128)(2,1)S(1)}, bf16[2,128,256]{2,1,0:T(8,128)(2,1)S(1)}, u32[]{:S(2)}, u32[]{:S(2)}) collective-permute-start(bf16[2,128,256]{2,1,0:T(8,128)(2,1)S(1)} %get-tuple-element.7), channel_id=1, source_target_pairs={{0,4},{2,6},{4,0},{6,2},{8,12},{10,14},{12,8},{14,10},{1,5},{3,7},... | collective-permute-start | bytes 393224 | tf_op jit(solution)/shard_map/ppermute | solution.py:29
  15.8 2.9 %collective-permute-done.1 = bf16[2,128,256]{2,1,0:T(8,128)(2,1)S(1)} collective-permute-done((bf16[2,128,256]{2,1,0:T(8,128)(2,1)S(1)}, bf16[2,128,256]{2,1,0:T(8,128)(2,1)S(1)}, u32[]{:S(2)}, u32[]{:S(2)}) %collective-permute-start.1) | collective-permute-done | bytes 131104 | tf_op jit(solution)/shard_map/ppermute | solution.py:29
  18.7 0.1 reverse_select_fusion.1
  18.8 3.1 %collective-permute-start.2 = (bf16[4,128,256]{2,1,0:T(8,128)(2,1)S(1)}, bf16[4,128,256]{2,1,0:T(8,128)(2,1)S(1)}, u32[]{:S(2)}, u32[]{:S(2)}) collective-permute-start(bf16[4,128,256]{2,1,0:T(8,128)(2,1)S(1)} %bitcast.78), channel_id=1, source_target_pairs={{0,8},{2,10},{4,12},{6,14},{8,0},{10,2},{12,4},{14,6},{1,9},{3,11}... | collective-permute-start | bytes 786440 | tf_op jit(solution)/shard_map/ppermute | solution.py:29
  21.9 9.6 %collective-permute-done.2 = bf16[4,128,256]{2,1,0:T(8,128)(2,1)S(1)} collective-permute-done((bf16[4,128,256]{2,1,0:T(8,128)(2,1)S(1)}, bf16[4,128,256]{2,1,0:T(8,128)(2,1)S(1)}, u32[]{:S(2)}, u32[]{:S(2)}) %collective-permute-start.2) | collective-permute-done | bytes 262176 | tf_op jit(solution)/shard_map/ppermute | solution.py:29
  31.5 0.1 pad_maximum_fusion
  31.6 0.1 reverse_select_fusion
  31.7 0.8 copy.15
  32.5 0.0 all-gather.2.cloned.1.call-update
  32.5 0.0 all-reduce.2.cloned.1.call-start
  32.6 0.7 compare_select_fusion
  33.3 0.7 compare_and_fusion
  34.0 9.0 %all-gather.2.cloned.1.call-done = bf16[256,2048]{1,0:T(8,128)(2,1)} async-done(((bf16[128,2048]{1,0:T(8,128)(2,1)}), bf16[256,2048]{1,0:T(8,128)(2,1)}) %all-gather.2.cloned.1.call-update) | async-done | bytes 1048592 | tf_op jit(solution)/shard_map/all_gather | solution.py:57
  42.9 3.7 %gather_fusion = bf16[256,2048]{1,0:T(8,128)(2,1)S(1)} fusion(bf16[256,2048]{1,0:T(8,128)(2,1)} %all-gather.2.cloned.1.call-done, s32[1024]{0:T(1024)S(1)} %pad_clamp_fusion), kind=kCustom, calls=%fused_computation | custom fusion | bytes 2098176 | tf_op jit(solution)/shard_map/jit(_take)/gather | solution.py:59
  46.7 0.0 copy-done
  46.7 0.0 copy-done.2
  46.7 5.8 %fusion.27 = f32[256,2048]{1,0:T(8,128)S(1)} fusion(bf16[1,2048,2048]{2,1,0:T(8,128)(2,1)} %param.12, f32[2048]{0:T(1024)S(1)} %bitcast.90, f32[2048]{0:T(1024)S(1)} %bitcast.82, bf16[256,2048]{1,0:T(8,128)(2,1)S(1)} %gather_fusion, pred[256]{0:T(512)(128)(4,1)S(1)} %compare_and_fusion), kind=kOutput, calls=%fused_computation.27 | convolution fusion | flops 2150105088 | bytes 11550976 | tf_op jit(solution)/shard_map/dot_general | solution.py:65
  52.5 0.0 copy-start.1
  52.5 7.0 %fusion.10 = f32[256,2048]{1,0:T(8,128)} fusion(bf16[1,2048,2048]{2,1,0:T(8,128)(2,1)} %param.14, f32[256,2048]{1,0:T(8,128)S(1)} %fusion.27), kind=kOutput, calls=%fused_computation.16 | convolution fusion | flops 2148532224 | bytes 12582912 | tf_op jit(solution)/shard_map/dot_general | solution.py:70
  59.5 0.0 all-reduce.2.cloned.1.call-update
  59.5 0.0 copy-done.1
  59.6 5.1 %multiply_reduce_fusion = f32[2048]{0:T(1024)S(1)} fusion(bf16[1,2048,2048]{2,1,0:T(8,128)(2,1)} %param.14), kind=kLoop, calls=%fused_computation.9 | loop fusion | flops 12580864 | bytes 8396800 | tf_op jit(solution)/shard_map/reduce_sum | solution.py:78
  64.7 97.9 %all-reduce.2.cloned.1.call-done = f32[256,2048]{1,0:T(8,128)} async-done(((f32[256,2048]{1,0:T(8,128)}), f32[256,2048]{1,0:T(8,128)}) %all-reduce.2.cloned.1.call-update) | async-done | bytes 2097168 | tf_op jit(solution)/shard_map/psum | solution.py:73
  162.6 14.7 %fusion.34 = f32[2048,2048]{1,0:T(8,128)} fusion(bf16[1,2048,2048]{2,1,0:T(8,128)(2,1)} %param.14, f32[256,2048]{1,0:T(8,128)S(1)} %fusion.27, f32[256,2048]{1,0:T(8,128)} %all-reduce.2.cloned.1.call-done, f32[2048]{0:T(1024)S(1)} %sqrt_multiply_fusion, f32[2048]{0:T(1024)S(1)} %bitcast.84, f32[2048]{0:T(1024)S(1)} %bitcast.83, ...), kind=kOutput, calls=%fused_computation.29 | convolution fusion | flops 4303355904 | bytes 30433536 | tf_op jit(solution)/shard_map/dot_general | solution.py:83
  177.3 27.9 %fusion.6 = (bf16[1,2048,2048]{2,1,0:T(8,128)(2,1)}, bf16[1,2048,2048]{2,1,0:T(8,128)(2,1)}, bf16[1,2048,2048]{2,1,0:T(8,128)(2,1)}) fusion(f32[2048,2048]{1,0:T(8,128)} %fusion.34, bf16[1,2048,2048]{2,1,0:T(8,128)(2,1)} %param.17, bf16[1,2048,2048]{2,1,0:T(8,128)(2,1)} %param.16, bf16[1,2048,2048]{2,1,0:T(8,128)(2,1)} %param.12), kind=kLoop, calls=%fused_computation.12 | loop fusion | flops 88080384 | bytes 67108864 | tf_op jit(solution)/shard_map/broadcast_in_dim | solution.py:92
  (5 shorter events, 0.1 us)
Async XLA Ops:
  7.2 39.5 %copy-start = (f32[1,2048]{1,0:T(1,128)S(1)}, f32[1,2048]{1,0:T(1,128)}, u32[]{:S(2)}) copy-start(f32[1,2048]{1,0:T(1,128)} %param.15) | copy-start | bytes 24580
  7.2 39.5 %copy-start.2 = (f32[1,2048]{1,0:T(1,128)S(1)}, f32[1,2048]{1,0:T(1,128)}, u32[]{:S(2)}) copy-start(f32[1,2048]{1,0:T(1,128)} %param.13) | copy-start | bytes 24580
  7.2 35.7 %all-gather.2.cloned.1.call-start = ((), (), s32[]{:S(2)}) async-start(), calls=%async_computation | async-start | bytes 1572864 | tf_op jit(solution)/shard_map/all_gather | solution.py:57
  7.2 5.5 %collective-permute-start = (bf16[1,128,256]{2,1,0:T(8,128)(2,1)}, bf16[1,128,256]{2,1,0:T(8,128)(2,1)S(1)}, u32[]{:S(2)}, u32[]{:S(2)}) collective-permute-start(bf16[1,128,256]{2,1,0:T(8,128)(2,1)} %bitcast.85), channel_id=1, source_target_pairs={{0,2},{2,0},{4,6},{6,4},{8,10},{10,8},{12,14},{14,12},{1,3},{3,1},... | collective-permute-start | bytes 196616 | tf_op jit(solution)/shard_map/ppermute | solution.py:29
  13.6 5.1 %collective-permute-start.1 = (bf16[2,128,256]{2,1,0:T(8,128)(2,1)S(1)}, bf16[2,128,256]{2,1,0:T(8,128)(2,1)S(1)}, u32[]{:S(2)}, u32[]{:S(2)}) collective-permute-start(bf16[2,128,256]{2,1,0:T(8,128)(2,1)S(1)} %get-tuple-element.7), channel_id=1, source_target_pairs={{0,4},{2,6},{4,0},{6,2},{8,12},{10,14},{12,8},{14,10},{1,5},{3,7},... | collective-permute-start | bytes 393224 | tf_op jit(solution)/shard_map/ppermute | solution.py:29
  18.8 12.7 %collective-permute-start.2 = (bf16[4,128,256]{2,1,0:T(8,128)(2,1)S(1)}, bf16[4,128,256]{2,1,0:T(8,128)(2,1)S(1)}, u32[]{:S(2)}, u32[]{:S(2)}) collective-permute-start(bf16[4,128,256]{2,1,0:T(8,128)(2,1)S(1)} %bitcast.78), channel_id=1, source_target_pairs={{0,8},{2,10},{4,12},{6,14},{8,0},{10,2},{12,4},{14,6},{1,9},{3,11}... | collective-permute-start | bytes 786440 | tf_op jit(solution)/shard_map/ppermute | solution.py:29
  32.5 130.0 %all-reduce.2.cloned.1.call-start = ((), (), s32[]{:S(2)}) async-start(), calls=%async_computation.1 | async-start | bytes 4194304 | tf_op jit(solution)/shard_map/psum | solution.py:73
  52.5 7.1 %copy-start.1 = (s32[1,2048]{1,0:T(1,128)S(1)}, s32[1,2048]{1,0:T(1,128)}, u32[]{:S(2)}) copy-start(s32[1,2048]{1,0:T(1,128)} %param.11) | copy-start | bytes 24580
Sparse Core Ops, SparseCore 0:
  32.7 10.2 all-gather.1
  59.6 102.8 all-reduce.1
